TPU v7x, 512 devices: a whole 4x4x16 slice. The times are simulated.
512 devices in a mesh: chan: 32 (over y, z_lo), inp: 16 (over z_hi, x, core).
Axes of the slice: x: 4, y: 4, z: 16 (z_hi: 2, z_lo: 8; z = z_hi * 8 + z_lo), core: 2. Of those that a mesh axis runs over, the one named last changes fastest.
Arguments:
- voltages: int32 [512, 524288], P('inp', 'chan'), may hold values from -128 to 127
- scales: int32 [512], P('inp'), may hold values from 1 to 5
Outputs:
- visibilities: bfloat16 [2, 1024, 512, 512], P(None, 'chan', 'inp')
All inputs are finite; a program needn't handle non-finite values.
Results may differ from a plain program's by a relative error of at most 0.0069.
Values may be sent and summed in bfloat16 or wider, within the bound.
No kernel may reach another device: no remote copies, remote signals or barrier semaphores. Data moves between devices by JAX's collectives and lax.ppermute only.
A program may use at most 128 MiB of HBM per device.

v0:
```python
import math
import jax
import jax.numpy as jnp
from jax import lax
from jax.sharding import PartitionSpec as P

NFFT = 4096
CHANS = 1024
TAPS = 8


def shifted(block, axis, distance):
    devices = range(lax.axis_size(axis))
    route = [(i - distance, i) for i in devices if i - distance in devices]
    return lax.ppermute(block, axis, route)


def window_table():
    count = TAPS * NFFT
    places = jnp.arange(count).astype(jnp.float32)
    shaping = jnp.sinc((places - count / 2.0) / NFFT)
    taper = 0.5 - 0.5 * jnp.cos(2.0 * math.pi * places / count)
    return (shaping * taper).reshape(TAPS, NFFT)


def dft_table():
    columns = jnp.arange(CHANS, dtype=jnp.int32)
    norm_factor = 1.0 / math.sqrt(NFFT)

    def one_block(start):
        rows_idx = start + jnp.arange(512, dtype=jnp.int32)
        phase = rows_idx[:, None] * columns[None, :] % NFFT
        angle = phase.astype(jnp.float32) * (2.0 * math.pi / NFFT)
        return jnp.stack(
            [jnp.cos(angle) * norm_factor, -jnp.sin(angle) * norm_factor], axis=1
        ).astype(jnp.bfloat16)

    starts = jnp.arange(NFFT // 512, dtype=jnp.int32) * 512
    return lax.map(one_block, starts).reshape(NFFT, 2, CHANS)


def filter_taps(padded, window, spec_count):
    total = jnp.zeros((padded.shape[0], spec_count, NFFT), jnp.float32)
    for tap_index in range(TAPS):
        total = total + window[tap_index] * padded[:, tap_index : tap_index + spec_count]
    return total.astype(jnp.bfloat16)


def shards(voltages, scales):
    inp_count = voltages.shape[0]
    shard_len = voltages.shape[1]
    spec_count = shard_len // NFFT
    history_len = (TAPS - 1) * NFFT
    reach_back = -(-history_len // shard_len)
    samples = voltages.astype(jnp.bfloat16)
    earlier = []
    for distance in range(1, reach_back + 1):
        take_count = min(shard_len, history_len - (distance - 1) * shard_len)
        received = shifted(samples[:, shard_len - take_count :], "chan", distance)
        earlier = [received] + earlier
    joined = jnp.concatenate(earlier + [samples], axis=1).astype(jnp.float32)
    signal = joined * scales.astype(jnp.float32)[:, None] * (1.0 / 256.0)
    padded = signal.reshape(inp_count, TAPS - 1 + spec_count, NFFT)
    filtered = filter_taps(padded, window_table(), spec_count)
    spectra = jnp.einsum(
        "isn,nrc->cirs", filtered, dft_table(), preferred_element_type=jnp.float32
    ).astype(jnp.bfloat16)
    local_block = lax.all_to_all(spectra, "chan", split_axis=0, concat_axis=3, tiled=True)
    chan_count = local_block.shape[0]
    spec_total = local_block.shape[3]
    own_rows = local_block.reshape(chan_count, inp_count, 2 * spec_total)
    swapped = jnp.concatenate([own_rows[..., spec_total:], -own_rows[..., :spec_total]], axis=-1)
    piece = lax.all_gather(own_rows, "inp", axis=1, tiled=True)
    real_part = jnp.einsum("cik,cjk->cij", own_rows, piece, preferred_element_type=jnp.float32)
    imag_part = jnp.einsum("cik,cjk->cij", swapped, piece, preferred_element_type=jnp.float32)
    result = jnp.stack([real_part, imag_part]) * (1.0 / spec_total)
    return result.astype(jnp.bfloat16)


def solution(mesh):
    placed = (P("inp", "chan"), P("inp"))
    return jax.shard_map(
        shards, mesh=mesh, in_specs=placed, out_specs=P(None, "chan", "inp", None), check_vma=False
    )
```

profile of v0, /device:TPU:1, one launch (start us, length us, event | category | flops | bytes accessed | tf_op | source)
XLA Modules:
  0.0 408.2 jit_solution(11215632262744515466)
XLA Ops:
  6.5 1.7 convert_element_type.91
  8.2 4.4 %collective-permute-start.1 = (bf16[32,16384]{1,0:T(8,128)(2,1)S(1)}, bf16[32,16384]{1,0:T(8,128)(2,1)S(1)}, u32[]{:S(2)}, u32[]{:S(2)}) collective-permute-start(bf16[32,16384]{1,0:T(8,128)(2,1)S(1)} %convert_element_type.91), channel_id=1, source_target_pairs={{0,16},{16,32},{32,48},{48,64},{64,80},{80,96},{96,112},{112,128},... | collective-permute-start | bytes 3145736 | tf_op jit(solution)/shard_map/ppermute | solution.py:15
  13.6 4.9 %collective-permute-start = (bf16[32,12288]{1,0:T(8,128)(2,1)}, bf16[32,12288]{1,0:T(8,128)(2,1)S(1)}, u32[]{:S(2)}, u32[]{:S(2)}) collective-permute-start(bf16[32,12288]{1,0:T(8,128)(2,1)} %slice.85), channel_id=1, source_target_pairs={{0,32},{16,48},{32,64},{48,80},{64,96},{80,112},{96,128},{112,144}... | collective-permute-start | bytes 2359304 | tf_op jit(solution)/shard_map/ppermute | solution.py:15
  18.5 95.0 %while.13 = (s32[]{:T(128)}, bf16[8,512,2,1024]{3,1,0,2:T(8,128)(2,1)}, s32[8]{0:T(128)S(1)}, s32[]{:T(128)}) while((s32[]{:T(128)}, bf16[8,512,2,1024]{3,1,0,2:T(8,128)(2,1)}, s32[8]{0:T(128)S(1)}, s32[]{:T(128)}) %tuple.40), condition=%wide.region_1.2_spmd.clone, body=%wide.region_0.1_spmd.clone.sunk | while | flops 14156290 | bytes 6295633 | solution.py:39
  19.8 9.1 %fusion.48 = (bf16[1,512,1,1024]{3,1,2,0:T(8,128)(2,1)S(1)}, bf16[1,512,1,1024]{3,1,2,0:T(8,128)(2,1)S(1)}) fusion(s32[512]{0:T(512)S(1)} %iota_add_fusion.2), kind=kLoop, calls=%fused_computation.15.clone.1 | loop fusion | flops 9961472 | bytes 2099200 | tf_op jit(solution)/shard_map/while/body/eval_jaxpr/stack | solution.py:34
  28.9 1.6 fusion.49
  31.7 9.1 %fusion.48 = (bf16[1,512,1,1024]{3,1,2,0:T(8,128)(2,1)S(1)}, bf16[1,512,1,1024]{3,1,2,0:T(8,128)(2,1)S(1)}) fusion(s32[512]{0:T(512)S(1)} %iota_add_fusion.2), kind=kLoop, calls=%fused_computation.15.clone.1 | loop fusion | flops 9961472 | bytes 2099200 | tf_op jit(solution)/shard_map/while/body/eval_jaxpr/stack | solution.py:34
  40.8 1.5 fusion.49
  43.6 9.1 %fusion.48 = (bf16[1,512,1,1024]{3,1,2,0:T(8,128)(2,1)S(1)}, bf16[1,512,1,1024]{3,1,2,0:T(8,128)(2,1)S(1)}) fusion(s32[512]{0:T(512)S(1)} %iota_add_fusion.2), kind=kLoop, calls=%fused_computation.15.clone.1 | loop fusion | flops 9961472 | bytes 2099200 | tf_op jit(solution)/shard_map/while/body/eval_jaxpr/stack | solution.py:34
  52.7 1.5 fusion.49
  55.5 9.1 %fusion.48 = (bf16[1,512,1,1024]{3,1,2,0:T(8,128)(2,1)S(1)}, bf16[1,512,1,1024]{3,1,2,0:T(8,128)(2,1)S(1)}) fusion(s32[512]{0:T(512)S(1)} %iota_add_fusion.2), kind=kLoop, calls=%fused_computation.15.clone.1 | loop fusion | flops 9961472 | bytes 2099200 | tf_op jit(solution)/shard_map/while/body/eval_jaxpr/stack | solution.py:34
  64.6 1.5 fusion.49
  67.3 9.1 %fusion.48 = (bf16[1,512,1,1024]{3,1,2,0:T(8,128)(2,1)S(1)}, bf16[1,512,1,1024]{3,1,2,0:T(8,128)(2,1)S(1)}) fusion(s32[512]{0:T(512)S(1)} %iota_add_fusion.2), kind=kLoop, calls=%fused_computation.15.clone.1 | loop fusion | flops 9961472 | bytes 2099200 | tf_op jit(solution)/shard_map/while/body/eval_jaxpr/stack | solution.py:34
  76.4 1.5 fusion.49
  79.2 9.1 %fusion.48 = (bf16[1,512,1,1024]{3,1,2,0:T(8,128)(2,1)S(1)}, bf16[1,512,1,1024]{3,1,2,0:T(8,128)(2,1)S(1)}) fusion(s32[512]{0:T(512)S(1)} %iota_add_fusion.2), kind=kLoop, calls=%fused_computation.15.clone.1 | loop fusion | flops 9961472 | bytes 2099200 | tf_op jit(solution)/shard_map/while/body/eval_jaxpr/stack | solution.py:34
  88.3 1.5 fusion.49
  91.1 9.1 %fusion.48 = (bf16[1,512,1,1024]{3,1,2,0:T(8,128)(2,1)S(1)}, bf16[1,512,1,1024]{3,1,2,0:T(8,128)(2,1)S(1)}) fusion(s32[512]{0:T(512)S(1)} %iota_add_fusion.2), kind=kLoop, calls=%fused_computation.15.clone.1 | loop fusion | flops 9961472 | bytes 2099200 | tf_op jit(solution)/shard_map/while/body/eval_jaxpr/stack | solution.py:34
  102.9 9.1 %fusion.48 = (bf16[1,512,1,1024]{3,1,2,0:T(8,128)(2,1)S(1)}, bf16[1,512,1,1024]{3,1,2,0:T(8,128)(2,1)S(1)}) fusion(s32[512]{0:T(512)S(1)} %iota_add_fusion.2), kind=kLoop, calls=%fused_computation.15.clone.1 | loop fusion | flops 9961472 | bytes 2099200 | tf_op jit(solution)/shard_map/while/body/eval_jaxpr/stack | solution.py:34
  112.0 1.5 fusion.49
  114.1 2.9 maximum_convert_fusion
  117.1 6.8 %reshape.221 = f32[32,11,4096]{2,1,0:T(8,128)} reshape(f32[32,45056]{1,0:T(8,128)} %maximum_convert_fusion) | data formatting | bytes 11534336 | tf_op jit(solution)/shard_map/convert_element_type | solution.py:61
  123.9 8.3 %multiply_multiply_fusion = f32[32,11,4096]{2,1,0:T(8,128)} fusion(f32[32,11,4096]{2,1,0:T(8,128)} %reshape.221, f32[32]{0:T(128)S(1)} %convert_element_type.94), kind=kLoop, calls=%fused_computation.18 | loop fusion | flops 2883584 | bytes 11534464 | tf_op jit(solution)/shard_map/mul | solution.py:62
  132.2 18.0 %fusion.13 = bf16[32,4,4096]{2,1,0:T(4,128)(2,1)S(1)} fusion(f32[32,11,4096]{2,1,0:T(8,128)} %multiply_multiply_fusion, f32[4096]{0:T(1024)S(1)} %get-tuple-element.79, f32[4096]{0:T(1024)S(1)} %get-tuple-element.80, f32[4096]{0:T(1024)S(1)} %get-tuple-element.81, f32[4096]{0:T(1024)S(1)} %get-tuple-element.82, f32[4096]{0:T(1024)S(1)} %get-tuple-element.83, ...), kind=kLoop, calls=%fused_computation.24 | loop fusion | flops 8388608 | bytes 17956864 | tf_op jit(solution)/shard_map/convert_element_type | solution.py:46
  150.2 8.7 %fusion.20 = bf16[1024,32,2,4]{0,1,3,2:T(8,128)(2,1)S(1)} fusion(bf16[4096,2,1024,1]{2,0,3,1:T(8,128)(2,1)} %bitcast.42, bf16[32,4,4096]{2,1,0:T(4,128)(2,1)S(1)} %fusion.13), kind=kOutput, calls=%fused_computation.41 | convolution fusion | flops 2147745792 | bytes 18350080 | tf_op jit(solution)/shard_map/isn,nrc->cirs/dot_general | solution.py:65
  160.3 2.0 reshape.224
  162.3 40.3 %all_to_all.15 = bf16[32,2,4096]{2,1,0:T(2,128)(2,1)S(1)} all-to-all(bf16[32,2,4096]{2,1,0:T(2,128)(2,1)S(1)} %reshape.224), channel_id=1, replica_groups=mesh['chan'=32,'inp'=16] {'chan'}, dimensions={0} | all-to-all | bytes 1048576 | tf_op jit(solution)/shard_map/all_to_all | solution.py:68
  203.6 1.9 copy.23
  205.5 3.4 copy.25
  210.0 180.6 %all-gather.2.cloned.1.call-done = bf16[32,512,256]{2,1,0:T(8,128)(2,1)} async-done(((bf16[32,32,256]{2,1,0:T(8,128)(2,1)}), bf16[32,512,256]{2,1,0:T(8,128)(2,1)}) %all-gather.2.cloned.1.call-update) | async-done | bytes 8388624 | tf_op jit(solution)/shard_map/all_gather | solution.py:73
  390.6 6.2 %convolution_bitcast_fusion.1 = f32[1,32,32,512]{3,2,1,0:T(8,128)S(1)} fusion(bf16[32,32,256]{2,1,0:T(8,128)(2,1)} %copy.25, bf16[32,512,256]{2,1,0:T(8,128)(2,1)} %all-gather.2.cloned.1.call-done), kind=kOutput, calls=%fused_computation.39 | convolution fusion | flops 268435456 | bytes 11010048 | tf_op jit(solution)/shard_map/cik,cjk->cij/dot_general | solution.py:74
  396.9 2.5 convolution_bitcast_fusion
  399.4 2.0 fusion.11
  (34 shorter events, 16.7 us)
Async XLA Ops:
  6.5 384.1 %all-gather.2.cloned.1.call-start = ((), (), s32[]{:S(2)}) async-start(), calls=%async_computation.1 | async-start | bytes 8912896 | tf_op jit(solution)/shard_map/all_gather | solution.py:73
  8.2 105.9 %collective-permute-start.1 = (bf16[32,16384]{1,0:T(8,128)(2,1)S(1)}, bf16[32,16384]{1,0:T(8,128)(2,1)S(1)}, u32[]{:S(2)}, u32[]{:S(2)}) collective-permute-start(bf16[32,16384]{1,0:T(8,128)(2,1)S(1)} %convert_element_type.91), channel_id=1, source_target_pairs={{0,16},{16,32},{32,48},{48,64},{64,80},{80,96},{96,112},{112,128},... | collective-permute-start | bytes 3145736 | tf_op jit(solution)/shard_map/ppermute | solution.py:15
  13.6 100.5 %collective-permute-start = (bf16[32,12288]{1,0:T(8,128)(2,1)}, bf16[32,12288]{1,0:T(8,128)(2,1)S(1)}, u32[]{:S(2)}, u32[]{:S(2)}) collective-permute-start(bf16[32,12288]{1,0:T(8,128)(2,1)} %slice.85), channel_id=1, source_target_pairs={{0,32},{16,48},{32,64},{48,80},{64,96},{80,112},{96,128},{112,144}... | collective-permute-start | bytes 2359304 | tf_op jit(solution)/shard_map/ppermute | solution.py:15
  18.5 95.0 %copy-start.1 = (s32[32]{0:T(128)S(1)}, s32[32]{0:T(128)}, u32[]{:S(2)}) copy-start(s32[32]{0:T(128)} %param.5) | copy-start | bytes 388
  390.6 6.2 %copy-start = (bf16[32,512,256]{2,1,0:T(8,128)(2,1)S(1)}, bf16[32,512,256]{2,1,0:T(8,128)(2,1)}, u32[]{:S(2)}) copy-start(bf16[32,512,256]{2,1,0:T(8,128)(2,1)} %all-gather.2.cloned.1.call-done) | copy-start | bytes 25165828
Sparse Core Ops, SparseCore 0:
  209.1 181.5 all-gather.1
where the time goes:
time: 409 us; the launch traced here: 408 us
  waiting for transfers between devices  181 us (44%)
  other arithmetic  124 us (30%)
  blocking collectives  40.3 us (10%)
  local copies, waits for them, and re-layouts  22.7 us (6%)
  matrix products  17.4 us (4%)
  between operations  13.5 us (3%)
  starting transfers between devices  9.31 us (2%)
    all_gather x1, waiting for transfers between devices, shards(): piece = lax.all_gather(own_rows, 'inp', axis=1, tiled=True)  181 us
    another operation x8, other arithmetic, one_block(): jnp.stack([jnp.cos(angle) * norm_factor, -jnp.sin(angle) * norm_factor],...  72.7 us
    all_to_all x1, blocking collectives, shards(): lax.all_to_all(spectra, 'chan', split_axis=0, concat_axis=3, tiled=True)  40.3 us
    convert_element_type x1, other arithmetic, filter_taps(): return total.astype(jnp.bfloat16)  18 us
    dynamic_update_slice x8, other arithmetic, dft_table(): return lax.map(one_block, starts).reshape(NFFT, 2, CHANS)  12 us
    ppermute x2, starting transfers between devices, shifted(): return lax.ppermute(block, axis, route)  9.31 us
    dot_general x1, matrix products, shards(): jnp.einsum('isn,nrc->cirs', filtered, dft_table(), preferred_element_type...  8.68 us
    mul x1, other arithmetic, shards(): signal = joined * scales.astype(jnp.float32)[:, None] * (1.0 / 256.0)  8.31 us
  transfers between devices with their start and end apart: 3, of which 1 were waited for; matrix products, arithmetic and copies ran while one was open for 24% of the time, Pallas kernels for 0%

commit v1 on v0

--- a/solution.py
+++ b/solution.py
@@ -70,7 +70,9 @@
     spec_total = local_block.shape[3]
     own_rows = local_block.reshape(chan_count, inp_count, 2 * spec_total)
     swapped = jnp.concatenate([own_rows[..., spec_total:], -own_rows[..., :spec_total]], axis=-1)
-    piece = lax.all_gather(own_rows, "inp", axis=1, tiled=True)
+    piece = jnp.concatenate(
+        lax.all_to_all(jnp.stack([own_rows] * lax.axis_size("inp")), "inp", 0, 0), axis=1
+    )
     real_part = jnp.einsum("cik,cjk->cij", own_rows, piece, preferred_element_type=jnp.float32)
     imag_part = jnp.einsum("cik,cjk->cij", swapped, piece, preferred_element_type=jnp.float32)
     result = jnp.stack([real_part, imag_part]) * (1.0 / spec_total)

time: 409 us -> 660 us (1.61)
  the two profiles are of different devices: /device:TPU:1 before, /device:TPU:103 now
where the time goes in v1:
time: 660 us; the launch traced here: 659 us
  waiting for transfers between devices  424 us (64%)
  other arithmetic  123 us (19%)
  local copies, waits for them, and re-layouts  34 us (5%)
  blocking collectives  31 us (5%)
  starting transfers between devices  28.8 us (4%)
  matrix products  17.3 us (3%)
    all_to_all x1, waiting for transfers between devices, shards(): lax.all_to_all(jnp.stack([own_rows] * lax.axis_size('inp')), 'inp', 0, 0)  424 us
    another operation x8, other arithmetic, one_block(): jnp.stack([jnp.cos(angle) * norm_factor, -jnp.sin(angle) * norm_factor],...  72.7 us
    all_to_all x1, blocking collectives, shards(): lax.all_to_all(spectra, 'chan', split_axis=0, concat_axis=3, tiled=True)  31 us
    all_to_all x1, starting transfers between devices, shards(): lax.all_to_all(jnp.stack([own_rows] * lax.axis_size('inp')), 'inp', 0, 0)  19.1 us
    convert_element_type x1, other arithmetic, filter_taps(): return total.astype(jnp.bfloat16)  18.1 us
  transfers between devices with their start and end apart: 3, of which 1 were waited for; matrix products, arithmetic and copies ran while one was open for 15% of the time, Pallas kernels for 0%

profile of v1, /device:TPU:103, one launch (start us, length us, event | category | flops | bytes accessed | tf_op | source)
XLA Modules:
  0.0 659.0 jit_solution(10353528121187602507)
XLA Ops:
  0.0 1.7 convert_element_type.91
  1.7 4.8 collective-permute-start.1
  7.4 4.9 collective-permute-start
  12.3 94.6 %while.13 = (s32[]{:T(128)}, bf16[8,512,2,1024]{3,1,0,2:T(8,128)(2,1)}, s32[8]{0:T(128)S(1)}, s32[]{:T(128)}) while((s32[]{:T(128)}, bf16[8,512,2,1024]{3,1,0,2:T(8,128)(2,1)}, s32[8]{0:T(128)S(1)}, s32[]{:T(128)}) %tuple.40), condition=%wide.region_1.2_spmd.clone, body=%wide.region_0.1_spmd.clone.sunk | while | flops 14156290 | bytes 6295633 | solution.py:39
  13.6 9.1 %fusion.48 = (bf16[1,512,1,1024]{3,1,2,0:T(8,128)(2,1)S(1)}, bf16[1,512,1,1024]{3,1,2,0:T(8,128)(2,1)S(1)}) fusion(s32[512]{0:T(512)S(1)} %iota_add_fusion.2), kind=kLoop, calls=%fused_computation.15.clone.1 | loop fusion | flops 9961472 | bytes 2099200 | tf_op jit(solution)/shard_map/while/body/eval_jaxpr/stack | solution.py:34
  22.7 1.5 fusion.49
  25.4 9.1 %fusion.48 = (bf16[1,512,1,1024]{3,1,2,0:T(8,128)(2,1)S(1)}, bf16[1,512,1,1024]{3,1,2,0:T(8,128)(2,1)S(1)}) fusion(s32[512]{0:T(512)S(1)} %iota_add_fusion.2), kind=kLoop, calls=%fused_computation.15.clone.1 | loop fusion | flops 9961472 | bytes 2099200 | tf_op jit(solution)/shard_map/while/body/eval_jaxpr/stack | solution.py:34
  37.2 9.1 %fusion.48 = (bf16[1,512,1,1024]{3,1,2,0:T(8,128)(2,1)S(1)}, bf16[1,512,1,1024]{3,1,2,0:T(8,128)(2,1)S(1)}) fusion(s32[512]{0:T(512)S(1)} %iota_add_fusion.2), kind=kLoop, calls=%fused_computation.15.clone.1 | loop fusion | flops 9961472 | bytes 2099200 | tf_op jit(solution)/shard_map/while/body/eval_jaxpr/stack | solution.py:34
  46.3 1.5 fusion.49
  49.1 9.1 %fusion.48 = (bf16[1,512,1,1024]{3,1,2,0:T(8,128)(2,1)S(1)}, bf16[1,512,1,1024]{3,1,2,0:T(8,128)(2,1)S(1)}) fusion(s32[512]{0:T(512)S(1)} %iota_add_fusion.2), kind=kLoop, calls=%fused_computation.15.clone.1 | loop fusion | flops 9961472 | bytes 2099200 | tf_op jit(solution)/shard_map/while/body/eval_jaxpr/stack | solution.py:34
  58.2 1.5 fusion.49
  60.9 9.1 %fusion.48 = (bf16[1,512,1,1024]{3,1,2,0:T(8,128)(2,1)S(1)}, bf16[1,512,1,1024]{3,1,2,0:T(8,128)(2,1)S(1)}) fusion(s32[512]{0:T(512)S(1)} %iota_add_fusion.2), kind=kLoop, calls=%fused_computation.15.clone.1 | loop fusion | flops 9961472 | bytes 2099200 | tf_op jit(solution)/shard_map/while/body/eval_jaxpr/stack | solution.py:34
  70.0 1.5 fusion.49
  72.7 9.1 %fusion.48 = (bf16[1,512,1,1024]{3,1,2,0:T(8,128)(2,1)S(1)}, bf16[1,512,1,1024]{3,1,2,0:T(8,128)(2,1)S(1)}) fusion(s32[512]{0:T(512)S(1)} %iota_add_fusion.2), kind=kLoop, calls=%fused_computation.15.clone.1 | loop fusion | flops 9961472 | bytes 2099200 | tf_op jit(solution)/shard_map/while/body/eval_jaxpr/stack | solution.py:34
  84.5 9.1 %fusion.48 = (bf16[1,512,1,1024]{3,1,2,0:T(8,128)(2,1)S(1)}, bf16[1,512,1,1024]{3,1,2,0:T(8,128)(2,1)S(1)}) fusion(s32[512]{0:T(512)S(1)} %iota_add_fusion.2), kind=kLoop, calls=%fused_computation.15.clone.1 | loop fusion | flops 9961472 | bytes 2099200 | tf_op jit(solution)/shard_map/while/body/eval_jaxpr/stack | solution.py:34
  96.3 9.1 %fusion.48 = (bf16[1,512,1,1024]{3,1,2,0:T(8,128)(2,1)S(1)}, bf16[1,512,1,1024]{3,1,2,0:T(8,128)(2,1)S(1)}) fusion(s32[512]{0:T(512)S(1)} %iota_add_fusion.2), kind=kLoop, calls=%fused_computation.15.clone.1 | loop fusion | flops 9961472 | bytes 2099200 | tf_op jit(solution)/shard_map/while/body/eval_jaxpr/stack | solution.py:34
  107.6 2.9 maximum_convert_fusion
  110.5 6.8 %reshape.232 = f32[32,11,4096]{2,1,0:T(8,128)} reshape(f32[32,45056]{1,0:T(8,128)} %maximum_convert_fusion) | data formatting | bytes 11534336 | tf_op jit(solution)/shard_map/convert_element_type | solution.py:61
  117.3 8.3 %multiply_multiply_fusion = f32[32,11,4096]{2,1,0:T(8,128)} fusion(f32[32,11,4096]{2,1,0:T(8,128)} %reshape.232, f32[32]{0:T(128)S(1)} %convert_element_type.94), kind=kLoop, calls=%fused_computation.18 | loop fusion | flops 2883584 | bytes 11534464 | tf_op jit(solution)/shard_map/mul | solution.py:62
  125.6 18.1 %fusion.13 = bf16[32,4,4096]{2,1,0:T(4,128)(2,1)S(1)} fusion(f32[32,11,4096]{2,1,0:T(8,128)} %multiply_multiply_fusion, f32[4096]{0:T(1024)S(1)} %get-tuple-element.79, f32[4096]{0:T(1024)S(1)} %get-tuple-element.80, f32[4096]{0:T(1024)S(1)} %get-tuple-element.81, f32[4096]{0:T(1024)S(1)} %get-tuple-element.82, f32[4096]{0:T(1024)S(1)} %get-tuple-element.83, ...), kind=kLoop, calls=%fused_computation.24 | loop fusion | flops 8388608 | bytes 17956864 | tf_op jit(solution)/shard_map/convert_element_type | solution.py:46
  143.8 8.7 %fusion.20 = bf16[1024,32,2,4]{0,1,3,2:T(8,128)(2,1)S(1)} fusion(bf16[4096,2,1024,1]{2,0,3,1:T(8,128)(2,1)} %bitcast.46, bf16[32,4,4096]{2,1,0:T(4,128)(2,1)S(1)} %fusion.13), kind=kOutput, calls=%fused_computation.41 | convolution fusion | flops 2147745792 | bytes 18350080 | tf_op jit(solution)/shard_map/isn,nrc->cirs/dot_general | solution.py:65
  153.9 2.0 reshape.235
  155.9 31.0 %all_to_all.20 = bf16[32,2,4096]{2,1,0:T(2,128)(2,1)S(1)} all-to-all(bf16[32,2,4096]{2,1,0:T(2,128)(2,1)S(1)} %reshape.235), channel_id=1, replica_groups=mesh['chan'=32,'inp'=16] {'chan'}, dimensions={0} | all-to-all | bytes 1048576 | tf_op jit(solution)/shard_map/all_to_all | solution.py:68
  187.9 1.9 copy.23
  189.8 2.8 copy.26
  192.5 4.3 stack.21
  196.9 19.1 %all-to-all-start.1 = ((bf16[16,32,32,256]{3,2,1,0:T(8,128)(2,1)}), bf16[16,32,32,256]{3,2,1,0:T(8,128)(2,1)}, u32[]{:S(2)}, u32[]{:S(2)}) async-start(bf16[16,32,32,256]{3,2,1,0:T(8,128)(2,1)} %stack.21), calls=%async_computation.1 | async-start | bytes 16777216 | tf_op jit(solution)/shard_map/all_to_all | solution.py:74
  216.1 424.3 %all-to-all-done.1 = bf16[16,32,32,256]{3,2,1,0:T(8,128)(2,1)} async-done(((bf16[16,32,32,256]{3,2,1,0:T(8,128)(2,1)}), bf16[16,32,32,256]{3,2,1,0:T(8,128)(2,1)}, u32[]{:S(2)}, u32[]{:S(2)}) %all-to-all-start.1) | async-done | bytes 8388640 | tf_op jit(solution)/shard_map/all_to_all | solution.py:74
  640.3 8.1 %copy.25 = bf16[32,16,32,256]{3,2,1,0:T(8,128)(2,1)} copy(bf16[32,16,32,256]{3,2,0,1:T(8,128)(2,1)} %bitcast.9) | data formatting | bytes 16777216 | tf_op jit(solution)/shard_map/reshape | solution.py:73
  648.4 6.1 convolution_bitcast_fusion.1
  654.5 2.5 convolution_bitcast_fusion
  657.0 2.0 fusion.11
  (35 shorter events, 19.7 us)
Async XLA Ops:
  1.7 105.9 %collective-permute-start.1 = (bf16[32,16384]{1,0:T(8,128)(2,1)S(1)}, bf16[32,16384]{1,0:T(8,128)(2,1)S(1)}, u32[]{:S(2)}, u32[]{:S(2)}) collective-permute-start(bf16[32,16384]{1,0:T(8,128)(2,1)S(1)} %convert_element_type.91), channel_id=1, source_target_pairs={{0,16},{16,32},{32,48},{48,64},{64,80},{80,96},{96,112},{112,128},... | collective-permute-start | bytes 3145736 | tf_op jit(solution)/shard_map/ppermute | solution.py:15
  7.4 100.2 %collective-permute-start = (bf16[32,12288]{1,0:T(8,128)(2,1)}, bf16[32,12288]{1,0:T(8,128)(2,1)S(1)}, u32[]{:S(2)}, u32[]{:S(2)}) collective-permute-start(bf16[32,12288]{1,0:T(8,128)(2,1)} %slice.85), channel_id=1, source_target_pairs={{0,32},{16,48},{32,64},{48,80},{64,96},{80,112},{96,128},{112,144}... | collective-permute-start | bytes 2359304 | tf_op jit(solution)/shard_map/ppermute | solution.py:15
  12.3 94.6 %copy-start.1 = (s32[32]{0:T(128)S(1)}, s32[32]{0:T(128)}, u32[]{:S(2)}) copy-start(s32[32]{0:T(128)} %param.5) | copy-start | bytes 388
  196.9 443.5 %all-to-all-start.1 = ((bf16[16,32,32,256]{3,2,1,0:T(8,128)(2,1)}), bf16[16,32,32,256]{3,2,1,0:T(8,128)(2,1)}, u32[]{:S(2)}, u32[]{:S(2)}) async-start(bf16[16,32,32,256]{3,2,1,0:T(8,128)(2,1)} %stack.21), calls=%async_computation.1 | async-start | bytes 16777216 | tf_op jit(solution)/shard_map/all_to_all | solution.py:74
  648.4 6.1 copy-start
